TPU v7x, 256 devices: a whole 4x4x8 slice. The times are simulated.
256 devices in a mesh: section: 4 (over z_hi, core), ep: 64 (over y, x, z_lo).
Axes of the slice: x: 4, y: 4, z: 8 (z_hi: 2, z_lo: 4; z = z_hi * 4 + z_lo), core: 2. Of those that a mesh axis runs over, the one named last changes fastest.
Arguments:
- tokens: bfloat16 [4, 8192, 4096], P('section', 'ep'), may hold values from -6 to 6
- routes: int32 [4, 8192, 8], P('section', 'ep'), may hold values from 0 to 127, as said below
- router_weights: float32 [4, 8192, 8], P('section', 'ep'), may hold values from 0.25 to 1
- w_gate: bfloat16 [4, 64, 4096, 384], P('section', 'ep'), may hold values from -0.09375 to 0.09375
- w_up: bfloat16 [4, 64, 4096, 384], P('section', 'ep'), may hold values from -0.09375 to 0.09375
- w_down: bfloat16 [4, 64, 384, 4096], P('section', 'ep'), may hold values from -0.15625 to 0.15625
- w_query: bfloat16 [4, 4096, 1024], P('section', 'ep'), may hold values from -0.09375 to 0.09375
- w_keyval: bfloat16 [4, 4096, 256], P('section', 'ep'), may hold values from -0.09375 to 0.09375
- gain_query: float32 [4, 128], P('section'), may hold values from 0.8 to 2
- gain_key: float32 [4, 128], P('section'), may hold values from 0.8 to 2
- segment_ids: int32 [4, 8192], P('section', 'ep'), may hold values from 0 to 31, never falling along the last dimension, each value on 1 to 512 neighbouring positions
Outputs:
- layer_out: bfloat16 [4, 8192, 4096], P('section', 'ep')
- attended: bfloat16 [4, 8192, 1024], P('section', 'ep')
Inputs may be any that keep to these rules, and one draw needn't show every extreme that they name: `routes`: each token names 8 different experts, at most one of them below 16. Among the tokens of one device (aligned blocks of 128 rows in each section) no expert below 16 is named by more than 8 of them, and in each section one expert below 16 is named by exactly 8 tokens of every block. `segment_ids`: along each section's tokens the reaction numbers never fall; each reaction spans 1 to 512 tokens and one spans exactly 512.
All inputs are finite; a program needn't handle non-finite values.
Results may differ from a plain program's by a relative error of at most 0.018.
Values may be sent and summed in bfloat16 or wider, within the bound.
No kernel may reach another device: no remote copies, remote signals or barrier semaphores. Data moves between devices by JAX's collectives and lax.ppermute only.
A program may use at most 128 MiB of HBM per device.

v0:
```python
import math
import jax
import jax.numpy as jnp
from jax import lax
from jax.sharding import PartitionSpec as P

OWNERS = 4
SEG_MOST = 512
EPSILON = 1e-06
ROPE_BASE = 1000000.0
FAR_INDEX = 1073741824


def passed_along(block, axis, distance):
    devices = range(lax.axis_size(axis))
    route = [((i - distance) % len(devices), i) for i in devices]
    return lax.ppermute(block, axis, route)


def prefix(shard, axis, combine, identity):
    length, mine = (lax.axis_size(axis), lax.axis_index(axis))
    everything = jax.tree.map(lambda part: lax.all_gather(part, axis), shard)
    start = jax.tree.map(
        lambda part, zero: jnp.broadcast_to(jnp.asarray(zero, part.dtype), part.shape),
        shard,
        identity,
    )

    def step(k, before):
        reached = k < mine
        new = combine(before, jax.tree.map(lambda part: part[k], everything))
        return jax.tree.map(lambda a, b: jnp.where(reached, a, b), new, before)

    return lax.fori_loop(0, length, step, start)


def passed_along_2(value, axis, steps):
    count = lax.axis_size(axis)
    leading, last = (max(0, -steps), min(count, count - steps))
    return lax.ppermute(value, axis, [(source, source + steps) for source in range(leading, last)])


def rms_rows(values):
    return values * lax.rsqrt(jnp.mean(values * values, axis=-1, keepdims=True) + EPSILON)


def rotary(values, position):
    half_count = values.shape[-1] // 2
    frequency = ROPE_BASE ** (-(jnp.arange(half_count, dtype=jnp.float32) * 2.0) / values.shape[-1])
    angles = position.astype(jnp.float32)[:, None] * frequency[None, :]
    cosine = jnp.concatenate([jnp.cos(angles), jnp.cos(angles)], axis=-1)[:, None, :]
    sine = jnp.concatenate([jnp.sin(angles), jnp.sin(angles)], axis=-1)[:, None, :]
    turned = jnp.concatenate([-values[..., half_count:], values[..., :half_count]], axis=-1)
    return values * cosine + turned * sine


def feed_forward(row_block, gate_part, up_part, down_part):
    gate_proj = jnp.dot(row_block, gate_part, preferred_element_type=jnp.float32)
    up_proj = jnp.dot(row_block, up_part, preferred_element_type=jnp.float32)
    activated = (jax.nn.silu(gate_proj) * up_proj).astype(jnp.bfloat16)
    return jnp.dot(activated, down_part, preferred_element_type=jnp.float32)


def keep_later(earlier, later):
    same_id = earlier[0] == later[0]
    newer_id = later[0] > earlier[0]
    start_at = jnp.where(
        same_id, jnp.minimum(earlier[1], later[1]), jnp.where(newer_id, later[1], earlier[1])
    )
    return (jnp.maximum(earlier[0], later[0]), start_at)


def on_device(
    tokens,
    routes,
    router_weights,
    w_gate,
    w_up,
    w_down,
    w_query,
    w_keyval,
    gain_query,
    gain_key,
    segment_ids,
):
    device_count = lax.axis_size("ep")
    expert_count = device_count // OWNERS
    token_count = tokens.shape[1]
    model_width = tokens.shape[2]
    capacity = OWNERS * max(1, token_count // device_count)
    wide_tokens = tokens[0].astype(jnp.float32)
    normed = rms_rows(wide_tokens).astype(jnp.bfloat16)
    inside = routes[0] < expert_count
    has_route = jnp.any(inside, axis=-1)
    chosen = jnp.sum(jnp.where(inside, routes[0], 0), axis=-1)
    weight_kept = jnp.sum(jnp.where(inside, router_weights[0], 0.0), axis=-1)
    expert_ids = jnp.arange(expert_count, dtype=jnp.int32)
    member = ((chosen[:, None] == expert_ids[None, :]) & has_route[:, None]).astype(jnp.int32)
    rank_within = jnp.sum((jnp.cumsum(member, axis=0) - member) * member, axis=-1)
    slot_index = jnp.where(has_route, chosen * capacity + rank_within, -1)
    slot_ids = jnp.arange(expert_count * capacity, dtype=jnp.int32)
    placing = (slot_ids[:, None] == slot_index[None, :]).astype(jnp.bfloat16)
    packed = jnp.dot(placing, normed, preferred_element_type=jnp.float32).astype(jnp.bfloat16)
    gate_part = w_gate[0, 0]
    up_part = w_up[0, 0]
    down_part = w_down[0, 0]
    spread = jnp.broadcast_to(
        packed.reshape(expert_count, 1, capacity, model_width),
        (expert_count, OWNERS, capacity, model_width),
    ).reshape(device_count, capacity, model_width)
    received = lax.all_to_all(spread, "ep", split_axis=0, concat_axis=0, tiled=True)
    partial_out = feed_forward(
        received.reshape(-1, model_width), gate_part, up_part, down_part
    ).reshape(received.shape)
    returned_rows = lax.all_to_all(
        partial_out.astype(jnp.bfloat16), "ep", split_axis=0, concat_axis=0, tiled=True
    ).astype(partial_out.dtype)
    merged = jnp.sum(
        returned_rows.reshape(expert_count, OWNERS, capacity, model_width), axis=1
    ).reshape(expert_count * capacity, model_width)
    fetched_rows = jnp.take(merged, jnp.maximum(slot_index, 0), axis=0)
    expert_out = jnp.where(has_route[:, None], fetched_rows, 0.0)
    layer_out = (wide_tokens + weight_kept[:, None] * expert_out).astype(jnp.bfloat16)
    arrived = passed_along(layer_out, "section", 1)
    lifted = rms_rows(arrived.astype(jnp.float32)).astype(jnp.bfloat16)
    head_dim = gain_query.shape[-1]
    query_width = w_query.shape[-1]
    head_count = query_width // head_dim
    query_raw = jnp.dot(
        lifted,
        lax.all_gather(w_query[0], "ep", axis=0, tiled=True),
        preferred_element_type=jnp.float32,
    )
    keyval_raw = jnp.dot(
        lifted,
        lax.all_gather(w_keyval[0], "ep", axis=0, tiled=True),
        preferred_element_type=jnp.float32,
    )
    segment_row = segment_ids[0]
    first_index = lax.axis_index("ep") * token_count
    global_index = first_index + jnp.arange(token_count, dtype=jnp.int32)
    reach = (SEG_MOST - 1) // token_count + 1
    key_index = (
        first_index - reach * token_count + jnp.arange((reach + 1) * token_count, dtype=jnp.int32)
    )
    segment_pieces = []
    for distance in range(1, reach + 1):
        segment_pieces.append(passed_along_2(segment_row, "ep", distance))
    window_segment = jnp.concatenate(segment_pieces[::-1] + [segment_row], axis=0)
    window_segment = jnp.where(key_index >= 0, window_segment, -1)
    same_segment = window_segment[None, :] == segment_row[:, None]
    start_index = jnp.min(jnp.where(same_segment, key_index[None, :], FAR_INDEX), axis=1)
    position = global_index - start_index
    query = rotary(
        rms_rows(query_raw.reshape(token_count, head_count, head_dim)) * gain_query[0], position
    ).astype(jnp.bfloat16)
    key_part = rotary(rms_rows(keyval_raw[:, None, :head_dim]) * gain_key[0], position)[
        :, 0
    ].astype(jnp.bfloat16)
    value_part = keyval_raw[:, head_dim:].astype(jnp.bfloat16)
    key_value = jnp.concatenate([key_part, value_part], axis=-1)
    earlier_pieces = []
    for distance in range(1, reach + 1):
        earlier_pieces.append(passed_along_2(key_value, "ep", distance))
    window = jnp.concatenate(earlier_pieces[::-1] + [key_value], axis=0)
    score_scale = 1.0 / math.sqrt(head_dim)
    scores = (
        jnp.einsum("thd,kd->thk", query, window[:, :head_dim], preferred_element_type=jnp.float32)
        * score_scale
    )
    allowed = (same_segment & (key_index[None, :] <= global_index[:, None]))[:, None, :]
    probabilities = jnp.where(allowed, jnp.exp(scores), 0.0)
    total_mass = jnp.sum(probabilities, axis=-1)
    mixed = jnp.einsum(
        "thk,kd->thd",
        probabilities.astype(jnp.bfloat16),
        window[:, head_dim:],
        preferred_element_type=jnp.float32,
    )
    attended = (
        (mixed / total_mass[..., None]).astype(jnp.bfloat16).reshape(token_count, query_width)
    )
    return (layer_out[None], attended[None])


def solution(mesh):
    in_specs = (
        P("section", "ep", None),
        P("section", "ep", None),
        P("section", "ep", None),
        P("section", "ep", None, None),
        P("section", "ep", None, None),
        P("section", "ep", None, None),
        P("section", "ep", None),
        P("section", "ep", None),
        P("section", None),
        P("section", None),
        P("section", "ep"),
    )
    out_specs = (P("section", "ep", None), P("section", "ep", None))
    return jax.shard_map(
        on_device, mesh=mesh, in_specs=in_specs, out_specs=out_specs, check_vma=False
    )
```

profile of v0, /device:TPU:32, one launch (start us, length us, event | category | flops | bytes accessed | tf_op | source)
XLA Modules:
  0.0 803.5 jit_solution(15481423913225358977)
XLA Ops:
  7.2 0.9 fusion.83
  8.0 0.8 fusion.79
  8.8 1.5 fusion.15
  10.8 1.7 fusion.2
  12.6 2.5 broadcast_in_dim.108
  15.0 11.8 %all-to-all-start = ((bf16[64,8,4096]{2,1,0:T(8,128)(2,1)}), bf16[64,8,4096]{2,1,0:T(8,128)(2,1)}, u32[]{:S(2)}, u32[]{:S(2)}) async-start(bf16[64,8,4096]{2,1,0:T(8,128)(2,1)} %bitcast.115), calls=%async_computation | async-start | bytes 8388608 | tf_op jit(solution)/shard_map/all_to_all | solution.py:111
  26.9 0.7 all-gather.7.cloned.1.call-update
  27.7 0.7 all-gather.5.cloned.1.call-update
  28.4 108.3 %all-to-all-done = bf16[64,8,4096]{2,1,0:T(8,128)(2,1)} async-done(((bf16[64,8,4096]{2,1,0:T(8,128)(2,1)}), bf16[64,8,4096]{2,1,0:T(8,128)(2,1)}, u32[]{:S(2)}, u32[]{:S(2)}) %all-to-all-start) | async-done | bytes 4194336 | tf_op jit(solution)/shard_map/all_to_all | solution.py:111
  136.7 6.4 fusion.5
  143.0 9.7 %convolution_convert_fusion = bf16[64,8,4096]{2,1,0:T(8,128)(2,1)} fusion(bf16[1,1,384,4096]{3,2,1,0:T(8,128)(2,1)S(1)} %copy-done, bf16[1,1,4096,384]{3,2,1,0:T(8,128)(2,1)} %param.15, bf16[64,8,4096]{2,1,0:T(8,128)(2,1)} %all-to-all-done, f32[512,384]{1,0:T(8,128)} %fusion.5), kind=kOutput, calls=%fused_computation.4 | convolution fusion | flops 3224502272 | bytes 15466496 | tf_op jit(solution)/shard_map/dot_general | solution.py:61
  152.8 6.9 all-to-all-start.1
  159.7 3.4 collective-permute-start
  163.0 3.4 collective-permute-start.1
  166.4 4.3 collective-permute-start.2
  170.7 4.3 collective-permute-start.3
  175.1 1.2 collective-permute-done
  176.3 32.1 %collective-permute-done.1 = s32[128]{0:T(128)S(1)} collective-permute-done((s32[128]{0:T(128)S(1)}, s32[128]{0:T(128)S(1)}, u32[]{:S(2)}, u32[]{:S(2)}) %collective-permute-start.1) | collective-permute-done | bytes 544 | tf_op jit(solution)/shard_map/ppermute | solution.py:40
  208.4 53.8 %collective-permute-done.2 = s32[128]{0:T(128)S(1)} collective-permute-done((s32[128]{0:T(128)S(1)}, s32[128]{0:T(128)S(1)}, u32[]{:S(2)}, u32[]{:S(2)}) %collective-permute-start.2) | collective-permute-done | bytes 544 | tf_op jit(solution)/shard_map/ppermute | solution.py:40
  262.8 7.9 all-to-all-done.1
  270.7 4.5 convert_reduce_fusion
  275.1 5.0 gather_fusion
  280.2 2.6 fusion.17
  283.2 1.6 fusion.18
  284.8 27.8 %collective-permute-done.4 = bf16[128,4096]{1,0:T(8,128)(2,1)S(1)} collective-permute-done((bf16[128,4096]{1,0:T(8,128)(2,1)S(1)}, bf16[128,4096]{1,0:T(8,128)(2,1)S(1)}, u32[]{:S(2)}, u32[]{:S(2)}) %collective-permute-start.4) | collective-permute-done | bytes 1048608 | tf_op jit(solution)/shard_map/ppermute | solution.py:17
  312.5 1.1 copy-done.3
  313.9 78.5 %all-gather.7.cloned.1.call-done = bf16[1,4096,256]{2,1,0:T(8,128)(2,1)} async-done(((bf16[1,64,256]{2,1,0:T(8,128)(2,1)}), bf16[1,4096,256]{2,1,0:T(8,128)(2,1)}) %all-gather.7.cloned.1.call-update) | async-done | bytes 2097168 | tf_op jit(solution)/shard_map/all_gather | solution.py:136
  392.4 2.4 fusion.21
  395.2 0.8 fusion.73
  396.0 1.9 collective-permute-start.5
  397.9 1.9 collective-permute-start.6
  399.8 1.9 collective-permute-start.7
  401.7 5.2 collective-permute-start.8
  406.9 373.2 %all-gather.5.cloned.1.call-done = bf16[1,4096,1024]{2,1,0:T(8,128)(2,1)} async-done(((bf16[1,64,1024]{2,1,0:T(8,128)(2,1)}), bf16[1,4096,1024]{2,1,0:T(8,128)(2,1)}) %all-gather.5.cloned.1.call-update) | async-done | bytes 8388624 | tf_op jit(solution)/shard_map/all_gather | solution.py:131
  780.1 5.0 fusion.43
  785.3 0.8 copy-done.4
  786.3 0.7 copy.19
  786.9 1.3 add_rsqrt_fusion
  788.2 0.8 copy.20
  789.0 1.3 multiply_multiply_fusion
  790.6 0.3 fusion.64
  790.9 0.8 constant_dynamic-update-slice_fusion.5
  791.8 0.8 constant_dynamic-update-slice_fusion.4
  792.6 0.8 constant_dynamic-update-slice_fusion.3
  793.5 0.8 constant_dynamic-update-slice_fusion.2
  794.3 0.8 fusion.13
  795.2 0.6 fusion.46
  795.8 0.9 copy.23
  (63 shorter events, 2.7 us)
Async XLA Ops:
  7.2 135.9 %copy-start = (bf16[1,1,384,4096]{3,2,1,0:T(8,128)(2,1)S(1)}, bf16[1,1,384,4096]{3,2,1,0:T(8,128)(2,1)}, u32[]{:S(2)}) copy-start(bf16[1,1,384,4096]{3,2,1,0:T(8,128)(2,1)} %param.16) | copy-start | bytes 9437188
  15.0 121.6 %all-to-all-start = ((bf16[64,8,4096]{2,1,0:T(8,128)(2,1)}), bf16[64,8,4096]{2,1,0:T(8,128)(2,1)}, u32[]{:S(2)}, u32[]{:S(2)}) async-start(bf16[64,8,4096]{2,1,0:T(8,128)(2,1)} %bitcast.115), calls=%async_computation | async-start | bytes 8388608 | tf_op jit(solution)/shard_map/all_to_all | solution.py:111
  26.9 365.5 %all-gather.7.cloned.1.call-start = ((), (), s32[]{:S(2)}) async-start(), calls=%async_computation.3 | async-start | bytes 2129920 | tf_op jit(solution)/shard_map/all_gather | solution.py:136
  27.6 752.5 %all-gather.5.cloned.1.call-start = ((), (), s32[]{:S(2)}) async-start(), calls=%async_computation.2 | async-start | bytes 8519680 | tf_op jit(solution)/shard_map/all_gather | solution.py:131
  152.8 6.9 copy-start.10
  152.8 22.3 %copy-start.6 = (s32[1,128,8]{1,2,0:T(8,128)S(1)}, s32[1,128,8]{1,2,0:T(8,128)}, u32[]{:S(2)}) copy-start(s32[1,128,8]{1,2,0:T(8,128)} %param.12) | copy-start | bytes 12292
  152.8 22.3 %copy-start.8 = (f32[1,128,8]{1,2,0:T(8,128)S(1)}, f32[1,128,8]{1,2,0:T(8,128)}, u32[]{:S(2)}) copy-start(f32[1,128,8]{1,2,0:T(8,128)} %param.13) | copy-start | bytes 12292
  152.8 117.9 %all-to-all-start.1 = ((bf16[64,8,4096]{2,1,0:T(8,128)(2,1)}), bf16[64,8,4096]{2,1,0:T(8,128)(2,1)}, u32[]{:S(2)}, u32[]{:S(2)}) async-start(bf16[64,8,4096]{2,1,0:T(8,128)(2,1)} %convolution_convert_fusion), calls=%async_computation.1 | async-start | bytes 8388608 | tf_op jit(solution)/shard_map/all_to_all | solution.py:115
  159.7 16.6 %collective-permute-start = (s32[128]{0:T(128)S(1)}, s32[128]{0:T(128)S(1)}, u32[]{:S(2)}, u32[]{:S(2)}) collective-permute-start(s32[128]{0:T(128)S(1)} %bitcast.120), channel_id=1, source_target_pairs={{0,4},{1,5},{2,6},{3,7},{4,8},{5,9},{6,10},{7,11},{8,12},{9,13},{1... | collective-permute-start | bytes 1544 | tf_op jit(solution)/shard_map/ppermute | solution.py:40
  163.0 45.4 %collective-permute-start.1 = (s32[128]{0:T(128)S(1)}, s32[128]{0:T(128)S(1)}, u32[]{:S(2)}, u32[]{:S(2)}) collective-permute-start(s32[128]{0:T(128)S(1)} %bitcast.121), channel_id=1, source_target_pairs={{0,3},{1,4},{2,5},{3,6},{4,7},{5,8},{6,9},{7,10},{8,11},{9,12},{10... | collective-permute-start | bytes 1544 | tf_op jit(solution)/shard_map/ppermute | solution.py:40
  166.4 95.8 %collective-permute-start.2 = (s32[128]{0:T(128)S(1)}, s32[128]{0:T(128)S(1)}, u32[]{:S(2)}, u32[]{:S(2)}) collective-permute-start(s32[128]{0:T(128)S(1)} %bitcast.122), channel_id=1, source_target_pairs={{0,2},{1,3},{2,4},{3,5},{4,6},{5,7},{6,8},{7,9},{8,10},{9,11},{10,... | collective-permute-start | bytes 1544 | tf_op jit(solution)/shard_map/ppermute | solution.py:40
  170.7 91.6 %collective-permute-start.3 = (s32[128]{0:T(128)S(1)}, s32[128]{0:T(128)S(1)}, u32[]{:S(2)}, u32[]{:S(2)}) collective-permute-start(s32[128]{0:T(128)S(1)} %bitcast.123), channel_id=1, source_target_pairs={{0,1},{1,2},{2,3},{3,4},{4,5},{5,6},{6,7},{7,8},{8,9},{9,10},{10,1... | collective-permute-start | bytes 1544 | tf_op jit(solution)/shard_map/ppermute | solution.py:40
  280.2 3.0 copy-start.1
  280.2 3.0 copy-start.2
  282.8 29.8 %collective-permute-start.4 = (bf16[128,4096]{1,0:T(8,128)(2,1)S(1)}, bf16[128,4096]{1,0:T(8,128)(2,1)S(1)}, u32[]{:S(2)}, u32[]{:S(2)}) collective-permute-start(bf16[128,4096]{1,0:T(8,128)(2,1)S(1)} %fusion.17), channel_id=1, source_target_pairs={{192,0},{0,64},{64,128},{128,192},{193,1},{1,65},{65,129},{129,193... | collective-permute-start | bytes 3145736 | tf_op jit(solution)/shard_map/ppermute | solution.py:17
  284.8 110.2 %copy-start.11 = (f32[1,128]{1,0:T(1,128)S(1)}, f32[1,128]{1,0:T(1,128)}, u32[]{:S(2)}) copy-start(f32[1,128]{1,0:T(1,128)} %param.20) | copy-start | bytes 1540
  312.5 1.1 copy-start.3
  313.9 78.5 %copy-start.7 = (f32[128]{0:T(128)}, f32[128]{0:T(128)S(1)}, u32[]{:S(2)}) copy-start(f32[128]{0:T(128)S(1)} %add_rsqrt_fusion.2) | copy-start | bytes 1540
  396.0 394.9 %collective-permute-start.5 = (bf16[128,256]{1,0:T(8,128)(2,1)S(1)}, bf16[128,256]{1,0:T(8,128)(2,1)}, u32[]{:S(2)}, u32[]{:S(2)}) collective-permute-start(bf16[128,256]{1,0:T(8,128)(2,1)S(1)} %pad_maximum_fusion.2), channel_id=1, source_target_pairs={{0,4},{1,5},{2,6},{3,7},{4,8},{5,9},{6,10},{7,11},{8,12},{9,13},{1... | collective-permute-start | bytes 196616 | tf_op jit(solution)/shard_map/ppermute | solution.py:40
  397.9 393.9 %collective-permute-start.6 = (bf16[128,256]{1,0:T(8,128)(2,1)S(1)}, bf16[128,256]{1,0:T(8,128)(2,1)}, u32[]{:S(2)}, u32[]{:S(2)}) collective-permute-start(bf16[128,256]{1,0:T(8,128)(2,1)S(1)} %pad_maximum_fusion.2), channel_id=1, source_target_pairs={{0,3},{1,4},{2,5},{3,6},{4,7},{5,8},{6,9},{7,10},{8,11},{9,12},{10... | collective-permute-start | bytes 196616 | tf_op jit(solution)/shard_map/ppermute | solution.py:40
  399.8 392.8 %collective-permute-start.7 = (bf16[128,256]{1,0:T(8,128)(2,1)S(1)}, bf16[128,256]{1,0:T(8,128)(2,1)}, u32[]{:S(2)}, u32[]{:S(2)}) collective-permute-start(bf16[128,256]{1,0:T(8,128)(2,1)S(1)} %pad_maximum_fusion.2), channel_id=1, source_target_pairs={{0,2},{1,3},{2,4},{3,5},{4,6},{5,7},{6,8},{7,9},{8,10},{9,11},{10,... | collective-permute-start | bytes 196616 | tf_op jit(solution)/shard_map/ppermute | solution.py:40
  401.7 391.7 %collective-permute-start.8 = (bf16[128,256]{1,0:T(8,128)(2,1)S(1)}, bf16[128,256]{1,0:T(8,128)(2,1)}, u32[]{:S(2)}, u32[]{:S(2)}) collective-permute-start(bf16[128,256]{1,0:T(8,128)(2,1)S(1)} %pad_maximum_fusion.2), channel_id=1, source_target_pairs={{0,1},{1,2},{2,3},{3,4},{4,5},{5,6},{6,7},{7,8},{8,9},{9,10},{10,1... | collective-permute-start | bytes 196616 | tf_op jit(solution)/shard_map/ppermute | solution.py:40
  785.2 0.8 copy-start.4
  789.0 1.5 copy-start.5
  789.0 1.5 copy-start.9
Sparse Core Ops, SparseCore 0:
  29.5 362.8 all-gather.6
  394.2 385.8 all-gather.4
where the time goes:
time: 804 us; the launch traced here: 803 us
  waiting for transfers between devices  684 us (85%)
  starting transfers between devices  45.3 us (6%)
  matrix products  26.7 us (3%)
  other arithmetic  17.7 us (2%)
  local copies, waits for them, and re-layouts  15.2 us (2%)
  between operations  14.4 us (2%)
    all_gather x1, waiting for transfers between devices, on_device(): lax.all_gather(w_query[0], 'ep', axis=0, tiled=True)  373 us
    all_to_all x1, waiting for transfers between devices, on_device(): lax.all_to_all(spread, 'ep', split_axis=0, concat_axis=0, tiled=True)  108 us
    ppermute x8, waiting for transfers between devices, passed_along_2(): lax.ppermute(value, axis, [(source, source + steps) for source in range(l...  87.2 us
    all_gather x1, waiting for transfers between devices, on_device(): lax.all_gather(w_keyval[0], 'ep', axis=0, tiled=True)  78.5 us
    ppermute x1, waiting for transfers between devices, passed_along(): return lax.ppermute(block, axis, route)  27.8 us
    ppermute x8, starting transfers between devices, passed_along_2(): lax.ppermute(value, axis, [(source, source + steps) for source in range(l...  26.2 us
  transfers between devices with their start and end apart: 13, of which 8 were waited for; matrix products, arithmetic and copies ran while one was open for 6% of the time, Pallas kernels for 0%

commit v1 on v0

--- a/solution.py
+++ b/solution.py
@@ -126,11 +126,13 @@
     head_dim = gain_query.shape[-1]
     query_width = w_query.shape[-1]
     head_count = query_width // head_dim
-    query_raw = jnp.dot(
-        lifted,
-        lax.all_gather(w_query[0], "ep", axis=0, tiled=True),
-        preferred_element_type=jnp.float32,
-    )
+
+    def fill_the_ports(slab_in):
+        return jnp.concatenate(
+            lax.all_to_all(jnp.stack([slab_in] * lax.psum(1, "ep")), "ep", 0, 0), axis=0
+        )
+
+    query_raw = jnp.dot(lifted, fill_the_ports(w_query[0]), preferred_element_type=jnp.float32)
     keyval_raw = jnp.dot(
         lifted,
         lax.all_gather(w_keyval[0], "ep", axis=0, tiled=True),

time: 804 us -> 661 us (0.82); the launches traced: 803 us -> 652 us
  waiting for transfers between devices: 684 us -> 340 us
  blocking collectives: 0 us -> 209 us
  starting transfers between devices: 45.3 us -> 26.9 us
    all_gather x1 -> x0, waiting for transfers between devices: 373 us -> none  [on_device(): lax.all_gather(w_query[0], 'ep', axis=0, tiled=True)]
    all_to_all x0 -> x2, blocking collectives: none -> 209 us  [the longest x1 108 us: on_device(): lax.all_to_all(spread, 'ep', split_axis=0, concat_axis=0, tiled=True)]
    all_to_all x2 -> x1, waiting for transfers between devices: 116 us -> 0.01 us  [fill_the_ports(): lax.all_to_all(jnp.stack([slab_in] * lax.psum(1, 'ep')), 'ep', 0, 0)]
    ppermute x8, waiting for transfers between devices: 87.2 us -> 201 us  [passed_along_2(): lax.ppermute(value, axis, [(source, source + steps) for source in range(l...]
    all_gather x1, waiting for transfers between devices: 78.5 us -> 130 us  [on_device(): lax.all_gather(w_keyval[0], 'ep', axis=0, tiled=True)]
    ppermute x1, waiting for transfers between devices: 27.8 us -> 9.49 us  [passed_along(): return lax.ppermute(block, axis, route)]
    all_to_all x2 -> x1, starting transfers between devices: 18.7 us -> 6.43 us  [fill_the_ports(): lax.all_to_all(jnp.stack([slab_in] * lax.psum(1, 'ep')), 'ep', 0, 0)]
    dot_general x0 -> x1, local copies, waits for them, and re-layouts: none -> 11.7 us  [on_device(): jnp.dot(lifted, fill_the_ports(w_query[0]), preferred_element_type=jnp.fl...]
  transfers between devices with their start and end apart: 13 -> 11, of which waited for: 8 -> 5; matrix products, arithmetic and copies ran while one was open for 6% -> 5% of each run, Pallas kernels for 0% -> 0%
where the time goes in v1:
time: 661 us; the launch traced here: 652 us
  waiting for transfers between devices  340 us (51%)
  blocking collectives  209 us (32%)
  starting transfers between devices  26.9 us (4%)
  matrix products  24.7 us (4%)
  local copies, waits for them, and re-layouts  22.6 us (3%)
  between operations  14.5 us (2%)
  other arithmetic  14.2 us (2%)
    ppermute x8, waiting for transfers between devices, passed_along_2(): lax.ppermute(value, axis, [(source, source + steps) for source in range(l...  201 us
    all_gather x1, waiting for transfers between devices, on_device(): lax.all_gather(w_keyval[0], 'ep', axis=0, tiled=True)  130 us
    all_to_all x1, blocking collectives, on_device(): lax.all_to_all(spread, 'ep', split_axis=0, concat_axis=0, tiled=True)  108 us
    all_to_all x1, blocking collectives, on_device(): lax.all_to_all(partial_out.astype(jnp.bfloat16), 'ep', split_axis=0, conc...  101 us
    ppermute x8, starting transfers between devices, passed_along_2(): lax.ppermute(value, axis, [(source, source + steps) for source in range(l...  20.4 us
  transfers between devices with their start and end apart: 11, of which 5 were waited for; matrix products, arithmetic and copies ran while one was open for 5% of the time, Pallas kernels for 0%

profile of v1, /device:TPU:32, one launch (start us, length us, event | category | flops | bytes accessed | tf_op | source)
XLA Modules:
  0.0 652.2 jit_solution(13211934177650480317)
XLA Ops:
  7.2 0.9 fusion.83
  8.0 0.8 fusion.78
  8.8 1.5 fusion.13
  10.4 0.1 fusion.74
  10.5 0.2 reduce_window_sum.11
  10.6 0.2 select_reduce_fusion
  10.8 1.7 fusion
  12.6 0.5 broadcast_in_dim.108
  13.1 107.7 %all_to_all.15 = bf16[64,8,4096]{2,1,0:T(8,128)(2,1)S(1)} all-to-all(bf16[64,8,4096]{2,1,0:T(8,128)(2,1)S(1)} %bitcast.116), channel_id=1, replica_groups=mesh['section'=4,'ep'=64] {'ep'}, dimensions={0} | all-to-all | bytes 8388608 | tf_op jit(solution)/shard_map/all_to_all | solution.py:111
  120.8 2.0 copy-done.4
  122.8 3.2 fusion.3
  126.0 9.7 %convolution_convert_fusion = bf16[64,8,4096]{2,1,0:T(8,128)(2,1)} fusion(bf16[1,1,384,4096]{3,2,1,0:T(8,128)(2,1)S(1)} %copy-done, bf16[1,1,4096,384]{3,2,1,0:T(8,128)(2,1)} %param.15, bf16[64,8,4096]{2,1,0:T(8,128)(2,1)} %copy-done.4, f32[512,384]{1,0:T(8,128)} %fusion.3), kind=kOutput, calls=%fused_computation.2 | convolution fusion | flops 3224502272 | bytes 15466496 | tf_op jit(solution)/shard_map/dot_general | solution.py:61
  135.7 101.0 %all_to_all.16 = bf16[64,8,4096]{2,1,0:T(8,128)(2,1)} all-to-all(bf16[64,8,4096]{2,1,0:T(8,128)(2,1)} %convolution_convert_fusion), channel_id=1, replica_groups=mesh['section'=4,'ep'=64] {'ep'}, dimensions={0} | all-to-all | bytes 8388608 | tf_op jit(solution)/shard_map/all_to_all | solution.py:115
  236.8 4.3 stack.3
  241.1 6.4 all-to-all-start.2
  247.5 3.4 collective-permute-start.3
  250.9 4.3 collective-permute-start.2
  255.2 3.4 collective-permute-start.1
  258.6 3.6 collective-permute-start
  262.3 19.4 %collective-permute-done = s32[128]{0:T(128)S(1)} collective-permute-done((s32[128]{0:T(128)S(1)}, s32[128]{0:T(128)S(1)}, u32[]{:S(2)}, u32[]{:S(2)}) %collective-permute-start) | collective-permute-done | bytes 544 | tf_op jit(solution)/shard_map/ppermute | solution.py:40
  281.8 62.0 %collective-permute-done.1 = s32[128]{0:T(128)S(1)} collective-permute-done((s32[128]{0:T(128)S(1)}, s32[128]{0:T(128)S(1)}, u32[]{:S(2)}, u32[]{:S(2)}) %collective-permute-start.1) | collective-permute-done | bytes 544 | tf_op jit(solution)/shard_map/ppermute | solution.py:40
  343.8 119.2 %collective-permute-done.2 = s32[128]{0:T(128)S(1)} collective-permute-done((s32[128]{0:T(128)S(1)}, s32[128]{0:T(128)S(1)}, u32[]{:S(2)}, u32[]{:S(2)}) %collective-permute-start.2) | collective-permute-done | bytes 544 | tf_op jit(solution)/shard_map/ppermute | solution.py:40
  463.1 0.2 fusion.65
  463.3 0.3 multiply_cosine_fusion
  463.6 3.2 convert_reduce_fusion
  466.8 2.6 gather_fusion
  469.4 3.1 fusion.15
  472.5 0.1 compare_and_fusion
  472.6 11.7 %copy.19 = bf16[1024,4096]{1,0:T(8,128)(2,1)} copy(bf16[1024,4096]{0,1:T(8,128)(2,1)} %bitcast.18) | data formatting | bytes 16777216 | tf_op jit(solution)/shard_map/dot_general | solution.py:135
  484.3 1.5 fusion.16
  485.8 9.5 %collective-permute-done.4 = bf16[128,4096]{1,0:T(8,128)(2,1)} collective-permute-done((bf16[128,4096]{1,0:T(8,128)(2,1)}, bf16[128,4096]{1,0:T(8,128)(2,1)}, u32[]{:S(2)}, u32[]{:S(2)}) %collective-permute-start.4) | collective-permute-done | bytes 1048608 | tf_op jit(solution)/shard_map/ppermute | solution.py:17
  495.3 1.5 fusion.17
  496.8 130.2 %all-gather.3.cloned.1.call-done = bf16[1,4096,256]{2,1,0:T(8,128)(2,1)} async-done(((bf16[1,64,256]{2,1,0:T(8,128)(2,1)}), bf16[1,4096,256]{2,1,0:T(8,128)(2,1)}) %all-gather.3.cloned.1.call-update) | async-done | bytes 2097168 | tf_op jit(solution)/shard_map/all_gather | solution.py:138
  627.1 2.4 fusion.19
  629.5 0.1 multiply_reduce_fusion.1
  629.8 0.1 fusion.72
  630.0 1.9 collective-permute-start.8
  631.9 1.3 collective-permute-start.7
  633.2 1.3 collective-permute-start.6
  634.5 1.3 collective-permute-start.5
  635.8 6.1 multiply_reduce_fusion
  642.0 0.1 multiply_multiply_fusion
  642.1 0.1 copy.20
  642.2 0.1 copy.21
  642.5 0.9 fusion.11
  643.4 0.6 fusion.41
  644.0 0.9 copy.24
  644.8 0.5 copy-done.1
  (59 shorter events, 0.5 us)
Async XLA Ops:
  7.2 118.9 %copy-start = (bf16[1,1,384,4096]{3,2,1,0:T(8,128)(2,1)S(1)}, bf16[1,1,384,4096]{3,2,1,0:T(8,128)(2,1)}, u32[]{:S(2)}) copy-start(bf16[1,1,384,4096]{3,2,1,0:T(8,128)(2,1)} %param.16) | copy-start | bytes 9437188
  13.1 109.7 %copy-start.11 = (bf16[1,1,4096,384]{3,2,1,0:T(8,128)(2,1)S(1)}, bf16[1,1,4096,384]{3,2,1,0:T(8,128)(2,1)}, u32[]{:S(2)}) copy-start(bf16[1,1,4096,384]{3,2,1,0:T(8,128)(2,1)} %param.14) | copy-start | bytes 9437188
  120.8 2.0 copy-start.4
  135.7 101.1 %copy-start.5 = (bf16[1,64,1024]{2,1,0:T(8,128)(2,1)S(1)}, bf16[1,64,1024]{2,1,0:T(8,128)(2,1)}, u32[]{:S(2)}) copy-start(bf16[1,64,1024]{2,1,0:T(8,128)(2,1)} %param.17) | copy-start | bytes 393220
  241.0 6.5 copy-start.8
  241.0 21.2 %copy-start.6 = (s32[1,128,8]{1,2,0:T(8,128)S(1)}, s32[1,128,8]{1,2,0:T(8,128)}, u32[]{:S(2)}) copy-start(s32[1,128,8]{1,2,0:T(8,128)} %param.12) | copy-start | bytes 12292
  241.0 21.2 %copy-start.7 = (f32[1,128,8]{1,2,0:T(8,128)S(1)}, f32[1,128,8]{1,2,0:T(8,128)}, u32[]{:S(2)}) copy-start(f32[1,128,8]{1,2,0:T(8,128)} %param.13) | copy-start | bytes 12292
  241.1 231.6 %all-to-all-start.2 = ((bf16[64,64,1024]{2,1,0:T(8,128)(2,1)}), bf16[64,64,1024]{2,1,0:T(8,128)(2,1)}, u32[]{:S(2)}, u32[]{:S(2)}) async-start(bf16[64,64,1024]{2,1,0:T(8,128)(2,1)} %stack.3), calls=%async_computation.2 | async-start | bytes 16777216 | tf_op jit(solution)/shard_map/all_to_all | solution.py:132
  247.5 379.6 %all-gather.3.cloned.1.call-start = ((), (), s32[]{:S(2)}) async-start(), calls=%async_computation.3 | async-start | bytes 2129920 | tf_op jit(solution)/shard_map/all_gather | solution.py:138
  247.5 215.5 %collective-permute-start.3 = (s32[128]{0:T(128)S(1)}, s32[128]{0:T(128)S(1)}, u32[]{:S(2)}, u32[]{:S(2)}) collective-permute-start(s32[128]{0:T(128)S(1)} %bitcast.119), channel_id=1, source_target_pairs={{0,1},{1,2},{2,3},{3,4},{4,5},{5,6},{6,7},{7,8},{8,9},{9,10},{10,1... | collective-permute-start | bytes 1544 | tf_op jit(solution)/shard_map/ppermute | solution.py:40
  250.9 212.1 %collective-permute-start.2 = (s32[128]{0:T(128)S(1)}, s32[128]{0:T(128)S(1)}, u32[]{:S(2)}, u32[]{:S(2)}) collective-permute-start(s32[128]{0:T(128)S(1)} %bitcast.120), channel_id=1, source_target_pairs={{0,2},{1,3},{2,4},{3,5},{4,6},{5,7},{6,8},{7,9},{8,10},{9,11},{10,... | collective-permute-start | bytes 1544 | tf_op jit(solution)/shard_map/ppermute | solution.py:40
  255.2 88.6 %collective-permute-start.1 = (s32[128]{0:T(128)S(1)}, s32[128]{0:T(128)S(1)}, u32[]{:S(2)}, u32[]{:S(2)}) collective-permute-start(s32[128]{0:T(128)S(1)} %bitcast.121), channel_id=1, source_target_pairs={{0,3},{1,4},{2,5},{3,6},{4,7},{5,8},{6,9},{7,10},{8,11},{9,12},{10... | collective-permute-start | bytes 1544 | tf_op jit(solution)/shard_map/ppermute | solution.py:40
  258.6 23.1 %collective-permute-start = (s32[128]{0:T(128)S(1)}, s32[128]{0:T(128)S(1)}, u32[]{:S(2)}, u32[]{:S(2)}) collective-permute-start(s32[128]{0:T(128)S(1)} %bitcast.122), channel_id=1, source_target_pairs={{0,4},{1,5},{2,6},{3,7},{4,8},{5,9},{6,10},{7,11},{8,12},{9,13},{1... | collective-permute-start | bytes 1544 | tf_op jit(solution)/shard_map/ppermute | solution.py:40
  466.8 2.6 copy-start.3
  472.5 22.8 %collective-permute-start.4 = (bf16[128,4096]{1,0:T(8,128)(2,1)}, bf16[128,4096]{1,0:T(8,128)(2,1)}, u32[]{:S(2)}, u32[]{:S(2)}) collective-permute-start(bf16[128,4096]{1,0:T(8,128)(2,1)} %fusion.15), channel_id=1, source_target_pairs={{192,0},{0,64},{64,128},{128,192},{193,1},{1,65},{65,129},{129,193... | collective-permute-start | bytes 3145736 | tf_op jit(solution)/shard_map/ppermute | solution.py:17
  472.6 11.7 %copy-start.2 = (f32[128,4096]{1,0:T(8,128)S(1)}, f32[128,4096]{1,0:T(8,128)}, u32[]{:S(2)}) copy-start(f32[128,4096]{1,0:T(8,128)} %gather_fusion) | copy-start | bytes 6291460
  485.8 143.8 %copy-start.9 = (f32[1,128]{1,0:T(1,128)S(1)}, f32[1,128]{1,0:T(1,128)}, u32[]{:S(2)}) copy-start(f32[1,128]{1,0:T(1,128)} %param.20) | copy-start | bytes 1540
  630.0 12.4 %collective-permute-start.8 = (bf16[128,256]{1,0:T(8,128)(2,1)S(1)}, bf16[128,256]{1,0:T(8,128)(2,1)S(1)}, u32[]{:S(2)}, u32[]{:S(2)}) collective-permute-start(bf16[128,256]{1,0:T(8,128)(2,1)S(1)} %pad_maximum_fusion.2), channel_id=1, source_target_pairs={{0,1},{1,2},{2,3},{3,4},{4,5},{5,6},{6,7},{7,8},{8,9},{9,10},{10,1... | collective-permute-start | bytes 196616 | tf_op jit(solution)/shard_map/ppermute | solution.py:40
  631.9 10.5 %collective-permute-start.7 = (bf16[128,256]{1,0:T(8,128)(2,1)S(1)}, bf16[128,256]{1,0:T(8,128)(2,1)S(1)}, u32[]{:S(2)}, u32[]{:S(2)}) collective-permute-start(bf16[128,256]{1,0:T(8,128)(2,1)S(1)} %pad_maximum_fusion.2), channel_id=1, source_target_pairs={{0,2},{1,3},{2,4},{3,5},{4,6},{5,7},{6,8},{7,9},{8,10},{9,11},{10,... | collective-permute-start | bytes 196616 | tf_op jit(solution)/shard_map/ppermute | solution.py:40
  633.2 9.2 %collective-permute-start.6 = (bf16[128,256]{1,0:T(8,128)(2,1)S(1)}, bf16[128,256]{1,0:T(8,128)(2,1)S(1)}, u32[]{:S(2)}, u32[]{:S(2)}) collective-permute-start(bf16[128,256]{1,0:T(8,128)(2,1)S(1)} %pad_maximum_fusion.2), channel_id=1, source_target_pairs={{0,3},{1,4},{2,5},{3,6},{4,7},{5,8},{6,9},{7,10},{8,11},{9,12},{10... | collective-permute-start | bytes 196616 | tf_op jit(solution)/shard_map/ppermute | solution.py:40
  634.5 7.8 %collective-permute-start.5 = (bf16[128,256]{1,0:T(8,128)(2,1)S(1)}, bf16[128,256]{1,0:T(8,128)(2,1)S(1)}, u32[]{:S(2)}, u32[]{:S(2)}) collective-permute-start(bf16[128,256]{1,0:T(8,128)(2,1)S(1)} %pad_maximum_fusion.2), channel_id=1, source_target_pairs={{0,4},{1,5},{2,6},{3,7},{4,8},{5,9},{6,10},{7,11},{8,12},{9,13},{1... | collective-permute-start | bytes 196616 | tf_op jit(solution)/shard_map/ppermute | solution.py:40
  635.8 6.2 copy-start.10
  643.4 2.0 copy-start.1
Sparse Core Ops, SparseCore 0:
  262.4 364.6 all-gather.2
